TPU v7x, 256 devices: a whole 4x4x8 slice. The times are simulated.
256 devices in a mesh: ctx: 32 (over y, z), tp: 8 (over x, core).
Axes of the slice: x: 4, y: 4, z: 8, core: 2. Of those that a mesh axis runs over, the one named last changes fastest.
Arguments:
- tokens: bfloat16 [16384, 4096], P('ctx', 'tp'), may hold values from -6 to 6
- qkv_blocks: bfloat16 [3, 4, 1024, 1024], P(None, None, None, 'tp'), may hold values from -0.046875 to 0.046875
- out_blocks: bfloat16 [4, 1024, 1024], P(None, 'tp'), may hold values from -0.046875 to 0.046875
- mix_factors: float32 [4, 4, 4, 4], replicated, may hold values from -4 to 4
- head_gain: float32 [4, 1024], P(None, 'tp'), may hold values from 0.1 to 1.9
Outputs:
- layer_out: bfloat16 [16384, 4096], P('ctx', 'tp')
All inputs are finite; a program needn't handle non-finite values.
Results may differ from a plain program's by a relative error of at most 0.025.
Values may be sent and summed in bfloat16 or wider, within the bound.
No kernel may reach another device: no remote copies, remote signals or barrier semaphores. Data moves between devices by JAX's collectives and lax.ppermute only.
A program may use at most 128 MiB of HBM per device.

v0:
```python
import functools
import jax
import jax.numpy as jnp
from jax import lax
from jax.sharding import PartitionSpec as P

PHM = 4
SPAN = 128
HEAD = 128
BLOCK = 1024
epsilon = 1e-06


def ring_gather(value, axis, devices, size, stride):
    here = lax.axis_index(axis)
    slots = [value]
    for shift in range(1, size):
        pairs = []
        for i in range(devices):
            k = i // stride % size
            pairs.append((i, i + ((k + shift) % size - k) * stride))
        slots.append(lax.ppermute(value, axis, pairs))
    source = (here // stride % size - jnp.arange(size)) % size
    return (jnp.stack(slots).astype(jnp.float32), source)


def exclusive_prefix(value, axis, devices, row):
    here = lax.axis_index(axis)
    pos, col = (here % row, here // row)
    within, source = ring_gather(value.astype(jnp.bfloat16), axis, devices, row, 1)
    before = jnp.einsum("k,k...->...", (source < pos).astype(jnp.float32), within)
    row_total = jnp.sum(within, axis=0)
    cols = devices // row
    across, source = ring_gather(row_total.astype(jnp.bfloat16), axis, devices, cols, row)
    return before + jnp.einsum("k,k...->...", (source < col).astype(jnp.float32), across)


def fold_weights(blocks, mixing):
    terms, rows, cols = blocks.shape
    folded = None
    for term_index in range(terms):
        part = (
            mixing[term_index][:, None, :, None]
            * blocks[term_index].astype(jnp.float32)[None, :, None, :]
        )
        folded = part if folded is None else folded + part
    return folded.astype(jnp.bfloat16).reshape(PHM * rows, PHM * cols)


def on_device(ctx_devices, ctx_row, tokens, qkv_blocks, out_blocks, mix_factors, head_gain):
    col_width = qkv_blocks.shape[-1]
    w_qkv = jnp.concatenate([fold_weights(qkv_blocks[p], mix_factors[p]) for p in range(3)], axis=1)
    w_out = fold_weights(out_blocks, mix_factors[3])
    whole = lax.all_gather(tokens, "tp", axis=1, tiled=True)
    tok_rows = whole.shape[0]
    local_heads = PHM * col_width // HEAD
    nblk = tok_rows // SPAN
    qkv = jnp.dot(whole, w_qkv, preferred_element_type=jnp.float32).astype(jnp.bfloat16)

    def project(p):
        part = qkv[:, p * PHM * col_width : (p + 1) * PHM * col_width]
        return part.reshape(nblk, SPAN, local_heads, HEAD)

    key_heads = project(1)
    value_heads = project(2)
    states = jnp.einsum(
        "nshd,nshe->nhde", key_heads, value_heads, preferred_element_type=jnp.float32
    )
    totals = jnp.sum(states, axis=0)
    earlier_sum = exclusive_prefix(totals, "ctx", ctx_devices, ctx_row)
    query_heads = project(0)
    scores = jnp.einsum(
        "nshd,nthd->nhst", query_heads, key_heads, preferred_element_type=jnp.float32
    )
    causal = jnp.arange(SPAN)[:, None] >= jnp.arange(SPAN)[None, :]
    scores = jnp.where(causal[None, None], scores, 0.0).astype(jnp.bfloat16)
    within = jnp.einsum("nhst,nthe->nshe", scores, value_heads, preferred_element_type=jnp.float32)
    prefixes = [earlier_sum]
    for n in range(1, nblk):
        prefixes.append(prefixes[-1] + states[n - 1])
    prefix = jnp.stack(prefixes, axis=0)
    prefix_hi = prefix.astype(jnp.bfloat16)
    prefix_lo = (prefix - prefix_hi.astype(jnp.float32)).astype(jnp.bfloat16)
    carried_out = jnp.einsum(
        "nshd,nhde->nshe", query_heads, prefix_hi, preferred_element_type=jnp.float32
    ) + jnp.einsum("nshd,nhde->nshe", query_heads, prefix_lo, preferred_element_type=jnp.float32)
    combined = within + carried_out
    mean_sq = jnp.mean(combined * combined, axis=-1, keepdims=True)
    normed = combined * lax.rsqrt(mean_sq + epsilon) * head_gain
    attn = normed.astype(jnp.bfloat16).reshape(tok_rows, PHM * col_width)
    partial_value = jnp.dot(attn, w_out, preferred_element_type=jnp.float32)
    reduced = lax.psum_scatter(
        partial_value.astype(jnp.bfloat16), "tp", scatter_dimension=1, tiled=True
    )
    return reduced


def ctx_row_of(mesh):
    n = mesh.shape["ctx"]
    return 8 if n % 8 == 0 else n


def solution(mesh):
    placed = (P("ctx", "tp"), P(None, None, None, "tp"), P(None, "tp", None), P(), P(None, "tp"))
    return jax.shard_map(
        functools.partial(on_device, mesh.shape["ctx"], ctx_row_of(mesh)),
        mesh=mesh,
        in_specs=placed,
        out_specs=P("ctx", "tp"),
        check_vma=False,
    )
```

profile of v0, /device:TPU:8, one launch (start us, length us, event | category | flops | bytes accessed | tf_op | source)
XLA Modules:
  0.0 160.8 jit_solution(9527223819864626604)
XLA Ops:
  6.5 0.7 all-gather.2.cloned.1.call-update
  7.3 0.9 slice_bitcast_fusion.18
  8.2 2.2 %bitcast_convert_fusion.15 = (f32[1024,128]{1,0:T(8,128)S(1)}, f32[1024,128]{1,0:T(8,128)S(1)}, f32[1024,128]{1,0:T(8,128)S(1)}, f32[1024,128]{1,0:T(8,128)S(1)}...) fusion(bf16[3,4,1024,128]{3,2,1,0:T(8,128)(2,1)} %param.6), kind=kLoop, calls=%fused_computation.62 | loop fusion | flops 1572864 | bytes 9437184 | tf_op jit(solution)/shard_map/convert_element_type | solution.py:44
  10.4 9.1 %add_convert_fusion.1 = (bf16[4,1024,4,128]{3,2,1,0:T(4,128)(2,1)S(1)}, bf16[4,1024,4,128]{3,2,1,0:T(4,128)(2,1)S(1)}) fusion(f32[1024,128]{1,0:T(8,128)S(1)} %get-tuple-element.17, f32[4,4]{1,0:T(4,128)S(1)} %get-tuple-element.30, f32[1024,128]{1,0:T(8,128)S(1)} %get-tuple-element.18, f32[4,4]{1,0:T(4,128)S(1)} %get-tuple-element.31, ...), kind=kLoop, calls=%fused_computation.7 | loop fusion | flops 33554432 | bytes 12583424 | tf_op jit(solution)/shard_map/convert.17
  19.6 2.7 %copy.52 = bf16[512,8,4,128]{3,1,2,0:T(8,128)(2,1)} copy(bf16[512,8,4,128]{3,2,1,0:T(4,128)(2,1)S(1)} %bitcast.181) | data formatting | bytes 8388608
  22.2 2.6 %copy.53 = bf16[512,8,4,128]{3,1,2,0:T(8,128)(2,1)} copy(bf16[512,8,4,128]{3,2,1,0:T(4,128)(2,1)S(1)} %bitcast.180) | data formatting | bytes 8388608
  24.9 4.6 %add_convert_fusion.3 = bf16[4,1024,4,128]{3,2,1,0:T(4,128)(2,1)S(1)} fusion(f32[1024,128]{1,0:T(8,128)S(1)} %get-tuple-element.14, f32[4,4]{1,0:T(4,128)S(1)} %get-tuple-element.38, f32[1024,128]{1,0:T(8,128)S(1)} %get-tuple-element.15, f32[4,4]{1,0:T(4,128)S(1)} %get-tuple-element.39, f32[1024,128]{1,0:T(8,128)S(1)} %get-tuple-element.16, ...), kind=kLoop, calls=%fused_computation.9 | loop fusion | flops 16777216 | bytes 6291712 | tf_op jit(solution)/shard_map/convert.19
  29.5 2.7 %copy.54 = bf16[512,8,4,128]{3,1,2,0:T(8,128)(2,1)} copy(bf16[512,8,4,128]{3,2,1,0:T(4,128)(2,1)S(1)} %bitcast.182) | data formatting | bytes 8388608
  32.2 0.2 bitcast_convert_fusion.3
  32.4 4.8 %add_convert_fusion = bf16[4,128,4,1024]{3,2,1,0:T(4,128)(2,1)S(1)} fusion(f32[128,1024]{1,0:T(8,128)S(1)} %get-tuple-element.24, f32[4,4]{1,0:T(4,128)S(1)} %get-tuple-element.41, f32[128,1024]{1,0:T(8,128)S(1)} %get-tuple-element.25, f32[4,4]{1,0:T(4,128)S(1)} %get-tuple-element.42, f32[128,1024]{1,0:T(8,128)S(1)} %get-tuple-element.23, ...), kind=kLoop, calls=%fused_computation.6 | loop fusion | flops 16777216 | bytes 6291712 | tf_op jit(solution)/shard_map/convert_element_type | solution.py:47
  37.3 4.2 %copy.33 = bf16[64,8,4,1024]{3,1,2,0:T(8,128)(2,1)} copy(bf16[64,8,4,1024]{3,2,1,0:T(4,128)(2,1)S(1)} %bitcast.183) | data formatting | bytes 8388608
  41.5 5.1 %all-gather.2.cloned.1.call-done = bf16[512,4096]{1,0:T(8,128)(2,1)} async-done(((bf16[512,512]{1,0:T(8,128)(2,1)}), bf16[512,4096]{1,0:T(8,128)(2,1)}) %all-gather.2.cloned.1.call-update) | async-done | bytes 4194320 | tf_op jit(solution)/shard_map/all_gather | solution.py:54
  46.7 13.8 %fusion.9 = bf16[512,1536]{0,1:T(8,128)(2,1)} fusion(bf16[512,4096]{1,0:T(8,128)(2,1)} %all-gather.2.cloned.1.call-done, bf16[4096,512]{1,0:T(8,128)(2,1)} %bitcast.187, bf16[4096,512]{1,0:T(8,128)(2,1)} %bitcast.188, bf16[4096,512]{1,0:T(8,128)(2,1)} %bitcast.189), kind=kOutput, calls=%fused_computation.15 | convolution fusion | flops 6480986112 | bytes 18350080 | tf_op jit(solution)/shard_map/dot_general | solution.py:58
  60.5 1.5 fusion.65
  62.1 0.4 copy.15
  62.4 0.1 reshape.330
  62.6 0.3 fusion.66
  62.9 1.6 %collective-permute-start = (bf16[4,128,128]{2,1,0:T(8,128)(2,1)S(1)}, bf16[4,128,128]{2,1,0:T(8,128)(2,1)S(1)}, u32[]{:S(2)}, u32[]{:S(2)}) collective-permute-start(bf16[4,128,128]{2,1,0:T(8,128)(2,1)S(1)} %get-tuple-element.43), channel_id=1, source_target_pairs={{0,8},{8,16},{16,24},{24,32},{32,40},{40,48},{48,56},{56,0},{64,72... | collective-permute-start | bytes 393224 | tf_op jit(solution)/shard_map/ppermute | solution.py:22
  64.5 2.5 %collective-permute-start.1 = (bf16[4,128,128]{2,1,0:T(8,128)(2,1)S(1)}, bf16[4,128,128]{2,1,0:T(8,128)(2,1)S(1)}, u32[]{:S(2)}, u32[]{:S(2)}) collective-permute-start(bf16[4,128,128]{2,1,0:T(8,128)(2,1)S(1)} %get-tuple-element.43), channel_id=1, source_target_pairs={{0,16},{8,24},{16,32},{24,40},{32,48},{40,56},{48,0},{56,8},{64,80... | collective-permute-start | bytes 393224 | tf_op jit(solution)/shard_map/ppermute | solution.py:22
  67.1 2.9 %collective-permute-start.2 = (bf16[4,128,128]{2,1,0:T(8,128)(2,1)S(1)}, bf16[4,128,128]{2,1,0:T(8,128)(2,1)}, u32[]{:S(2)}, u32[]{:S(2)}) collective-permute-start(bf16[4,128,128]{2,1,0:T(8,128)(2,1)S(1)} %get-tuple-element.43), channel_id=1, source_target_pairs={{0,24},{8,32},{16,40},{24,48},{32,56},{40,0},{48,8},{56,16},{64,88... | collective-permute-start | bytes 393224 | tf_op jit(solution)/shard_map/ppermute | solution.py:22
  70.0 2.0 %collective-permute-start.3 = (bf16[4,128,128]{2,1,0:T(8,128)(2,1)S(1)}, bf16[4,128,128]{2,1,0:T(8,128)(2,1)}, u32[]{:S(2)}, u32[]{:S(2)}) collective-permute-start(bf16[4,128,128]{2,1,0:T(8,128)(2,1)S(1)} %get-tuple-element.43), channel_id=1, source_target_pairs={{0,32},{8,40},{16,48},{24,56},{32,0},{40,8},{48,16},{56,24},{64,96... | collective-permute-start | bytes 393224 | tf_op jit(solution)/shard_map/ppermute | solution.py:22
  72.0 3.1 %collective-permute-start.4 = (bf16[4,128,128]{2,1,0:T(8,128)(2,1)S(1)}, bf16[4,128,128]{2,1,0:T(8,128)(2,1)}, u32[]{:S(2)}, u32[]{:S(2)}) collective-permute-start(bf16[4,128,128]{2,1,0:T(8,128)(2,1)S(1)} %get-tuple-element.43), channel_id=1, source_target_pairs={{0,40},{8,48},{16,56},{24,0},{32,8},{40,16},{48,24},{56,32},{64,10... | collective-permute-start | bytes 393224 | tf_op jit(solution)/shard_map/ppermute | solution.py:22
  75.3 0.4 copy.17
  75.6 1.6 %fusion.15 = f32[4,4,128,128]{3,2,1,0:T(8,128)} fusion(bf16[4,128,4,128]{3,1,2,0:T(8,128)(2,1)S(1)} %copy.15, bf16[4,128,4,128]{3,1,2,0:T(8,128)(2,1)S(1)} %copy.17, pred[128,128]{1,0:T(8,128)(4,1)S(1)} %iota_compare_fusion, bf16[4,128,4,128]{1,0,3,2:T(4,128)(2,1)S(1)} %reshape.330), kind=kOutput, calls=%fused_computation.21 | convolution fusion | flops 134742016 | bytes 2637824 | tf_op jit(solution)/shard_map/nhst,nthe->nshe/dot_general | solution.py:77
  77.3 3.4 %collective-permute-start.5 = (bf16[4,128,128]{2,1,0:T(8,128)(2,1)S(1)}, bf16[4,128,128]{2,1,0:T(8,128)(2,1)S(1)}, u32[]{:S(2)}, u32[]{:S(2)}) collective-permute-start(bf16[4,128,128]{2,1,0:T(8,128)(2,1)S(1)} %get-tuple-element.43), channel_id=1, source_target_pairs={{0,48},{8,56},{16,0},{24,8},{32,16},{40,24},{48,32},{56,40},{64,11... | collective-permute-start | bytes 393224 | tf_op jit(solution)/shard_map/ppermute | solution.py:22
  80.7 1.4 collective-permute-start.6
  82.1 2.0 %collective-permute-done.2 = bf16[4,128,128]{2,1,0:T(8,128)(2,1)} collective-permute-done((bf16[4,128,128]{2,1,0:T(8,128)(2,1)S(1)}, bf16[4,128,128]{2,1,0:T(8,128)(2,1)}, u32[]{:S(2)}, u32[]{:S(2)}) %collective-permute-start.2) | collective-permute-done | bytes 131104 | tf_op jit(solution)/shard_map/ppermute | solution.py:22
  84.0 4.6 %collective-permute-done.3 = bf16[4,128,128]{2,1,0:T(8,128)(2,1)} collective-permute-done((bf16[4,128,128]{2,1,0:T(8,128)(2,1)S(1)}, bf16[4,128,128]{2,1,0:T(8,128)(2,1)}, u32[]{:S(2)}, u32[]{:S(2)}) %collective-permute-start.3) | collective-permute-done | bytes 131104 | tf_op jit(solution)/shard_map/ppermute | solution.py:22
  88.6 2.8 %collective-permute-done.4 = bf16[4,128,128]{2,1,0:T(8,128)(2,1)} collective-permute-done((bf16[4,128,128]{2,1,0:T(8,128)(2,1)S(1)}, bf16[4,128,128]{2,1,0:T(8,128)(2,1)}, u32[]{:S(2)}, u32[]{:S(2)}) %collective-permute-start.4) | collective-permute-done | bytes 131104 | tf_op jit(solution)/shard_map/ppermute | solution.py:22
  91.4 3.7 %collective-permute-done.5 = bf16[4,128,128]{2,1,0:T(8,128)(2,1)S(1)} collective-permute-done((bf16[4,128,128]{2,1,0:T(8,128)(2,1)S(1)}, bf16[4,128,128]{2,1,0:T(8,128)(2,1)S(1)}, u32[]{:S(2)}, u32[]{:S(2)}) %collective-permute-start.5) | collective-permute-done | bytes 131104 | tf_op jit(solution)/shard_map/ppermute | solution.py:22
  95.1 1.1 collective-permute-done.6
  96.2 1.1 add_add_fusion
  97.3 1.6 collective-permute-start.7
  98.8 1.1 collective-permute-start.8
  100.0 2.1 %collective-permute-start.9 = (bf16[4,128,128]{2,1,0:T(8,128)(2,1)S(1)}, bf16[4,128,128]{2,1,0:T(8,128)(2,1)S(1)}, u32[]{:S(2)}, u32[]{:S(2)}) collective-permute-start(bf16[4,128,128]{2,1,0:T(8,128)(2,1)S(1)} %add_add_fusion), channel_id=1, source_target_pairs={{0,192},{8,200},{16,208},{24,216},{32,224},{40,232},{48,240},{56,2... | collective-permute-start | bytes 393224 | tf_op jit(solution)/shard_map/ppermute | solution.py:22
  102.2 0.9 bitcast_dynamic-update-slice_fusion.4
  103.1 0.9 bitcast_dynamic-update-slice_fusion.3
  104.0 0.9 bitcast_dynamic-update-slice_fusion.2
  105.0 0.7 fusion.16
  105.8 0.2 collective-permute-done.8
  106.0 0.6 collective-permute-done.9
  106.7 0.5 fusion.22
  107.3 0.5 fusion.30
  107.8 0.5 multiply_reduce_fusion
  108.4 0.2 multiply_convert_fusion
  108.6 0.3 copy.20
  108.9 6.5 %convolution_convert_fusion = bf16[512,4096]{1,0:T(8,128)(2,1)} fusion(bf16[512,4096]{1,0:T(8,128)(2,1)} %bitcast.186, bf16[64,8,4,128]{3,2,1,0:T(4,128)(2,1)S(1)} %bitcast.191), kind=kOutput, calls=%fused_computation.10 | convolution fusion | flops 2149580800 | bytes 8912896 | tf_op jit(solution)/shard_map/dot_general | solution.py:91
  115.5 38.5 %reduce-scatter.2.cloned.1.call-done = bf16[512,512]{1,0:T(8,128)(2,1)} async-done(((bf16[512,4096]{1,0:T(8,128)(2,1)}), bf16[512,512]{1,0:T(8,128)(2,1)}) %reduce-scatter.2.cloned.1.call-update) | async-done | bytes 524304 | tf_op jit(solution)/shard_map/reduce_scatter | solution.py:92
  (24 shorter events, 0.6 us)
Async XLA Ops:
  6.5 40.1 %all-gather.2.cloned.1.call-start = ((), (), s32[]{:S(2)}) async-start(), calls=%async_computation.1 | async-start | bytes 4718592 | tf_op jit(solution)/shard_map/all_gather | solution.py:54
  7.3 146.7 %reduce-scatter.2.cloned.1.call-start = ((), (), s32[]{:S(2)}) async-start(), calls=%async_computation.2 | async-start | bytes 4718592 | tf_op jit(solution)/shard_map/reduce_scatter | solution.py:92
  29.5 2.7 %copy-start.1 = (bf16[4,128,1024]{2,1,0:T(8,128)(2,1)S(1)}, bf16[4,128,1024]{2,1,0:T(8,128)(2,1)}, u32[]{:S(2)}) copy-start(bf16[4,128,1024]{2,1,0:T(8,128)(2,1)} %param.7) | copy-start | bytes 3145732
  62.9 14.4 %collective-permute-start = (bf16[4,128,128]{2,1,0:T(8,128)(2,1)S(1)}, bf16[4,128,128]{2,1,0:T(8,128)(2,1)S(1)}, u32[]{:S(2)}, u32[]{:S(2)}) collective-permute-start(bf16[4,128,128]{2,1,0:T(8,128)(2,1)S(1)} %get-tuple-element.43), channel_id=1, source_target_pairs={{0,8},{8,16},{16,24},{24,32},{32,40},{40,48},{48,56},{56,0},{64,72... | collective-permute-start | bytes 393224 | tf_op jit(solution)/shard_map/ppermute | solution.py:22
  64.5 16.2 %collective-permute-start.1 = (bf16[4,128,128]{2,1,0:T(8,128)(2,1)S(1)}, bf16[4,128,128]{2,1,0:T(8,128)(2,1)S(1)}, u32[]{:S(2)}, u32[]{:S(2)}) collective-permute-start(bf16[4,128,128]{2,1,0:T(8,128)(2,1)S(1)} %get-tuple-element.43), channel_id=1, source_target_pairs={{0,16},{8,24},{16,32},{24,40},{32,48},{40,56},{48,0},{56,8},{64,80... | collective-permute-start | bytes 393224 | tf_op jit(solution)/shard_map/ppermute | solution.py:22
  67.1 17.0 %collective-permute-start.2 = (bf16[4,128,128]{2,1,0:T(8,128)(2,1)S(1)}, bf16[4,128,128]{2,1,0:T(8,128)(2,1)}, u32[]{:S(2)}, u32[]{:S(2)}) collective-permute-start(bf16[4,128,128]{2,1,0:T(8,128)(2,1)S(1)} %get-tuple-element.43), channel_id=1, source_target_pairs={{0,24},{8,32},{16,40},{24,48},{32,56},{40,0},{48,8},{56,16},{64,88... | collective-permute-start | bytes 393224 | tf_op jit(solution)/shard_map/ppermute | solution.py:22
  70.0 18.6 %collective-permute-start.3 = (bf16[4,128,128]{2,1,0:T(8,128)(2,1)S(1)}, bf16[4,128,128]{2,1,0:T(8,128)(2,1)}, u32[]{:S(2)}, u32[]{:S(2)}) collective-permute-start(bf16[4,128,128]{2,1,0:T(8,128)(2,1)S(1)} %get-tuple-element.43), channel_id=1, source_target_pairs={{0,32},{8,40},{16,48},{24,56},{32,0},{40,8},{48,16},{56,24},{64,96... | collective-permute-start | bytes 393224 | tf_op jit(solution)/shard_map/ppermute | solution.py:22
  72.0 19.4 %collective-permute-start.4 = (bf16[4,128,128]{2,1,0:T(8,128)(2,1)S(1)}, bf16[4,128,128]{2,1,0:T(8,128)(2,1)}, u32[]{:S(2)}, u32[]{:S(2)}) collective-permute-start(bf16[4,128,128]{2,1,0:T(8,128)(2,1)S(1)} %get-tuple-element.43), channel_id=1, source_target_pairs={{0,40},{8,48},{16,56},{24,0},{32,8},{40,16},{48,24},{56,32},{64,10... | collective-permute-start | bytes 393224 | tf_op jit(solution)/shard_map/ppermute | solution.py:22
  77.3 17.8 %collective-permute-start.5 = (bf16[4,128,128]{2,1,0:T(8,128)(2,1)S(1)}, bf16[4,128,128]{2,1,0:T(8,128)(2,1)S(1)}, u32[]{:S(2)}, u32[]{:S(2)}) collective-permute-start(bf16[4,128,128]{2,1,0:T(8,128)(2,1)S(1)} %get-tuple-element.43), channel_id=1, source_target_pairs={{0,48},{8,56},{16,0},{24,8},{32,16},{40,24},{48,32},{56,40},{64,11... | collective-permute-start | bytes 393224 | tf_op jit(solution)/shard_map/ppermute | solution.py:22
  80.7 15.5 %collective-permute-start.6 = (bf16[4,128,128]{2,1,0:T(8,128)(2,1)S(1)}, bf16[4,128,128]{2,1,0:T(8,128)(2,1)S(1)}, u32[]{:S(2)}, u32[]{:S(2)}) collective-permute-start(bf16[4,128,128]{2,1,0:T(8,128)(2,1)S(1)} %get-tuple-element.43), channel_id=1, source_target_pairs={{0,56},{8,0},{16,8},{24,16},{32,24},{40,32},{48,40},{56,48},{64,12... | collective-permute-start | bytes 393224 | tf_op jit(solution)/shard_map/ppermute | solution.py:22
  97.3 8.5 %collective-permute-start.7 = (bf16[4,128,128]{2,1,0:T(8,128)(2,1)S(1)}, bf16[4,128,128]{2,1,0:T(8,128)(2,1)S(1)}, u32[]{:S(2)}, u32[]{:S(2)}) collective-permute-start(bf16[4,128,128]{2,1,0:T(8,128)(2,1)S(1)} %add_add_fusion), channel_id=1, source_target_pairs={{0,64},{8,72},{16,80},{24,88},{32,96},{40,104},{48,112},{56,120},{... | collective-permute-start | bytes 393224 | tf_op jit(solution)/shard_map/ppermute | solution.py:22
  98.8 7.1 %collective-permute-start.8 = (bf16[4,128,128]{2,1,0:T(8,128)(2,1)S(1)}, bf16[4,128,128]{2,1,0:T(8,128)(2,1)S(1)}, u32[]{:S(2)}, u32[]{:S(2)}) collective-permute-start(bf16[4,128,128]{2,1,0:T(8,128)(2,1)S(1)} %add_add_fusion), channel_id=1, source_target_pairs={{0,128},{8,136},{16,144},{24,152},{32,160},{40,168},{48,176},{56,1... | collective-permute-start | bytes 393224 | tf_op jit(solution)/shard_map/ppermute | solution.py:22
  100.0 6.6 %collective-permute-start.9 = (bf16[4,128,128]{2,1,0:T(8,128)(2,1)S(1)}, bf16[4,128,128]{2,1,0:T(8,128)(2,1)S(1)}, u32[]{:S(2)}, u32[]{:S(2)}) collective-permute-start(bf16[4,128,128]{2,1,0:T(8,128)(2,1)S(1)} %add_add_fusion), channel_id=1, source_target_pairs={{0,192},{8,200},{16,208},{24,216},{32,224},{40,232},{48,240},{56,2... | collective-permute-start | bytes 393224 | tf_op jit(solution)/shard_map/ppermute | solution.py:22
  105.0 2.8 %copy-start = (f32[4,4,128,128]{3,2,1,0:T(8,128)S(1)}, f32[4,4,128,128]{3,2,1,0:T(8,128)}, u32[]{:S(2)}) copy-start(f32[4,4,128,128]{3,2,1,0:T(8,128)} %fusion.15) | copy-start | bytes 3145732
  107.2 1.2 copy-start.2
Sparse Core Ops, SparseCore 0:
  9.2 37.4 all-gather.1
  115.6 38.3 reduce-scatter.1
where the time goes:
time: 161 us
  waiting for transfers between devices  59.3 us (37%)
  matrix products  24.6 us (15%)
  other arithmetic  22.5 us (14%)
  starting transfers between devices  21.9 us (14%)
  local copies, waits for them, and re-layouts  18.9 us (12%)
  between operations  13.7 us (9%)
    reduce_scatter x1, waiting for transfers between devices, on_device(): lax.psum_scatter(partial_value.astype(jnp.bfloat16), 'tp', scatter_dimens...  38.5 us
    ppermute x10, starting transfers between devices, ring_gather(): slots.append(lax.ppermute(value, axis, pairs))  21.8 us
    unnamed x17, local copies, waits for them, and re-layouts  15.1 us
    ppermute x10, waiting for transfers between devices, ring_gather(): slots.append(lax.ppermute(value, axis, pairs))  15 us
    dot_general x1, matrix products, on_device(): jnp.dot(whole, w_qkv, preferred_element_type=jnp.float32)  13.8 us
    another operation x2, other arithmetic  13.7 us
    dot_general x1, matrix products, on_device(): partial_value = jnp.dot(attn, w_out, preferred_element_type=jnp.float32)  6.53 us
    all_gather x1, waiting for transfers between devices, on_device(): whole = lax.all_gather(tokens, 'tp', axis=1, tiled=True)  5.13 us
  transfers between devices with their start and end apart: 12, of which 9 were waited for; matrix products, arithmetic and copies ran while one was open for 25% of the time, Pallas kernels for 0%

commit v1 on v0

--- a/solution.py
+++ b/solution.py
@@ -51,7 +51,9 @@
     col_width = qkv_blocks.shape[-1]
     w_qkv = jnp.concatenate([fold_weights(qkv_blocks[p], mix_factors[p]) for p in range(3)], axis=1)
     w_out = fold_weights(out_blocks, mix_factors[3])
-    whole = lax.all_gather(tokens, "tp", axis=1, tiled=True)
+    whole = jnp.concatenate(
+        lax.all_to_all(jnp.stack([tokens] * lax.axis_size("tp")), "tp", 0, 0), axis=1
+    )
     tok_rows = whole.shape[0]
     local_heads = PHM * col_width // HEAD
     nblk = tok_rows // SPAN

time: 161 us -> 178 us (1.11)
  starting transfers between devices: 21.9 us -> 30.8 us
  waiting for transfers between devices: 59.3 us -> 63.6 us
  local copies, waits for them, and re-layouts: 18.9 us -> 22.7 us
    all_to_all x0 -> x1, waiting for transfers between devices: none -> 13.1 us  [on_device(): lax.all_to_all(jnp.stack([tokens] * lax.axis_size('tp')), 'tp', 0, 0)]
    all_gather x1 -> x0, waiting for transfers between devices: 5.13 us -> none  [on_device(): whole = lax.all_gather(tokens, 'tp', axis=1, tiled=True)]
    all_to_all x0 -> x1, starting transfers between devices: none -> 4.83 us  [on_device(): lax.all_to_all(jnp.stack([tokens] * lax.axis_size('tp')), 'tp', 0, 0)]
    ppermute x10, starting transfers between devices: 21.8 us -> 25.9 us  [ring_gather(): slots.append(lax.ppermute(value, axis, pairs))]
    unnamed x17 -> x32, local copies, waits for them, and re-layouts: 15.1 us -> 18.8 us
    ppermute x10, waiting for transfers between devices: 15 us -> 12.6 us  [ring_gather(): slots.append(lax.ppermute(value, axis, pairs))]
    another operation x0 -> x1, local copies, waits for them, and re-layouts: none -> 2.36 us  [on_device(): jnp.stack([tokens] * lax.axis_size('tp'))]
  transfers between devices with their start and end apart: 12 -> 12, of which waited for: 9 -> 8; matrix products, arithmetic and copies ran while one was open for 25% -> 24% of each run, Pallas kernels for 0% -> 0%
where the time goes in v1:
time: 178 us; the launch traced here: 177 us
  waiting for transfers between devices  63.6 us (36%)
  starting transfers between devices  30.8 us (17%)
  matrix products  23.3 us (13%)
  other arithmetic  23.2 us (13%)
  local copies, waits for them, and re-layouts  22.7 us (13%)
  between operations  13.7 us (8%)
    reduce_scatter x1, waiting for transfers between devices, on_device(): lax.psum_scatter(partial_value.astype(jnp.bfloat16), 'tp', scatter_dimens...  37.9 us
    ppermute x10, starting transfers between devices, ring_gather(): slots.append(lax.ppermute(value, axis, pairs))  25.9 us
    unnamed x32, local copies, waits for them, and re-layouts  18.8 us
    another operation x2, other arithmetic  14.9 us
    all_to_all x1, waiting for transfers between devices, on_device(): lax.all_to_all(jnp.stack([tokens] * lax.axis_size('tp')), 'tp', 0, 0)  13.1 us
    ppermute x10, waiting for transfers between devices, ring_gather(): slots.append(lax.ppermute(value, axis, pairs))  12.6 us
    dot_general x1, matrix products, on_device(): jnp.dot(whole, w_qkv, preferred_element_type=jnp.float32)  12.6 us
    dot_general x1, matrix products, on_device(): partial_value = jnp.dot(attn, w_out, preferred_element_type=jnp.float32)  6.49 us
  transfers between devices with their start and end apart: 12, of which 8 were waited for; matrix products, arithmetic and copies ran while one was open for 24% of the time, Pallas kernels for 0%

profile of v1, /device:TPU:8, one launch (start us, length us, event | category | flops | bytes accessed | tf_op | source)
XLA Modules:
  0.0 177.3 jit_solution(12167838803466493151)
XLA Ops:
  6.5 1.3 copy.13
  7.8 2.4 %stack.66 = bf16[8,512,512]{1,2,0:T(8,128)(2,1)} broadcast(bf16[512,512]{0,1:T(8,128)(2,1)S(1)} %copy.13), dimensions={1,2} | broadcast | bytes 4718592 | tf_op jit(solution)/shard_map/stack | solution.py:55
  10.2 4.8 %all-to-all-start = ((bf16[8,512,512]{1,2,0:T(8,128)(2,1)}), bf16[8,512,512]{1,2,0:T(8,128)(2,1)}, u32[]{:S(2)}, u32[]{:S(2)}) async-start(bf16[8,512,512]{1,2,0:T(8,128)(2,1)} %stack.66), calls=%async_computation | async-start | bytes 8388608 | tf_op jit(solution)/shard_map/all_to_all | solution.py:55
  15.1 1.7 bitcast_convert_fusion.15
  16.8 10.3 %add_convert_fusion.1 = (bf16[4,1024,4,128]{3,2,1,0:T(4,128)(2,1)}, bf16[4,1024,4,128]{3,2,1,0:T(4,128)(2,1)}) fusion(f32[1024,128]{1,0:T(8,128)S(1)} %get-tuple-element.17, f32[4,4]{1,0:T(4,128)S(1)} %get-tuple-element.30, f32[1024,128]{1,0:T(8,128)S(1)} %get-tuple-element.18, f32[4,4]{1,0:T(4,128)S(1)} %get-tuple-element.31, ...), kind=kLoop, calls=%fused_computation.7 | loop fusion | flops 33554432 | bytes 12583424 | tf_op jit(solution)/shard_map/convert.17
  27.1 5.0 %copy.53 = bf16[512,8,4,128]{3,1,2,0:T(8,128)(2,1)} copy(bf16[512,8,4,128]{3,2,1,0:T(4,128)(2,1)} %bitcast.184) | data formatting | bytes 8388608
  32.1 2.7 %copy.54 = bf16[512,8,4,128]{3,1,2,0:T(8,128)(2,1)} copy(bf16[512,8,4,128]{3,2,1,0:T(4,128)(2,1)S(1)} %bitcast.183) | data formatting | bytes 8388608
  34.8 4.6 %add_convert_fusion.3 = bf16[4,1024,4,128]{3,2,1,0:T(4,128)(2,1)S(1)} fusion(f32[1024,128]{1,0:T(8,128)S(1)} %copy-done.4, f32[4,4]{1,0:T(4,128)S(1)} %get-tuple-element.38, f32[1024,128]{1,0:T(8,128)S(1)} %copy-done.5, f32[4,4]{1,0:T(4,128)S(1)} %get-tuple-element.39, f32[1024,128]{1,0:T(8,128)S(1)} %copy-done.6, f32[4,4]{1,0:T(4,128)S(1)} %get-tuple-element.40, ...), kind=kLoop, calls=%fused_computation.9 | loop fusion | flops 16777216 | bytes 6291712 | tf_op jit(solution)/shard_map/convert.19
  39.5 2.7 %copy.55 = bf16[512,8,4,128]{3,1,2,0:T(8,128)(2,1)} copy(bf16[512,8,4,128]{3,2,1,0:T(4,128)(2,1)S(1)} %bitcast.185) | data formatting | bytes 8388608
  42.2 0.2 bitcast_convert_fusion.3
  42.4 4.8 %add_convert_fusion = bf16[4,128,4,1024]{3,2,1,0:T(4,128)(2,1)S(1)} fusion(f32[128,1024]{1,0:T(8,128)S(1)} %get-tuple-element.24, f32[4,4]{1,0:T(4,128)S(1)} %get-tuple-element.41, f32[128,1024]{1,0:T(8,128)S(1)} %get-tuple-element.25, f32[4,4]{1,0:T(4,128)S(1)} %get-tuple-element.42, f32[128,1024]{1,0:T(8,128)S(1)} %get-tuple-element.23, ...), kind=kLoop, calls=%fused_computation.6 | loop fusion | flops 16777216 | bytes 6291712 | tf_op jit(solution)/shard_map/convert_element_type | solution.py:47
  47.2 4.3 %copy.34 = bf16[64,8,4,1024]{3,1,2,0:T(8,128)(2,1)} copy(bf16[64,8,4,1024]{3,2,1,0:T(4,128)(2,1)S(1)} %bitcast.186) | data formatting | bytes 8388608
  51.5 13.1 %all-to-all-done = bf16[8,512,512]{1,2,0:T(8,128)(2,1)} async-done(((bf16[8,512,512]{1,2,0:T(8,128)(2,1)}), bf16[8,512,512]{1,2,0:T(8,128)(2,1)}, u32[]{:S(2)}, u32[]{:S(2)}) %all-to-all-start) | async-done | bytes 4194336 | tf_op jit(solution)/shard_map/all_to_all | solution.py:55
  64.6 12.6 %fusion.9 = bf16[512,1536]{0,1:T(8,128)(2,1)S(1)} fusion(bf16[512,4096]{0,1:T(8,128)(2,1)} %bitcast.25, bf16[4096,512]{1,0:T(8,128)(2,1)} %bitcast.190, bf16[4096,512]{1,0:T(8,128)(2,1)} %bitcast.191, bf16[4096,512]{1,0:T(8,128)(2,1)} %bitcast.192), kind=kOutput, calls=%fused_computation.15 | convolution fusion | flops 6480986112 | bytes 18350080 | tf_op jit(solution)/shard_map/dot_general | solution.py:60
  77.3 0.1 reshape.338
  77.5 0.4 copy.16
  77.9 0.1 reshape.340
  78.0 0.3 fusion.66
  78.3 2.0 %collective-permute-start = (bf16[4,128,128]{2,1,0:T(8,128)(2,1)S(1)}, bf16[4,128,128]{2,1,0:T(8,128)(2,1)S(1)}, u32[]{:S(2)}, u32[]{:S(2)}) collective-permute-start(bf16[4,128,128]{2,1,0:T(8,128)(2,1)S(1)} %get-tuple-element.43), channel_id=1, source_target_pairs={{0,8},{8,16},{16,24},{24,32},{32,40},{40,48},{48,56},{56,0},{64,72... | collective-permute-start | bytes 393224 | tf_op jit(solution)/shard_map/ppermute | solution.py:22
  80.3 3.3 %collective-permute-start.1 = (bf16[4,128,128]{2,1,0:T(8,128)(2,1)S(1)}, bf16[4,128,128]{2,1,0:T(8,128)(2,1)S(1)}, u32[]{:S(2)}, u32[]{:S(2)}) collective-permute-start(bf16[4,128,128]{2,1,0:T(8,128)(2,1)S(1)} %get-tuple-element.43), channel_id=1, source_target_pairs={{0,16},{8,24},{16,32},{24,40},{32,48},{40,56},{48,0},{56,8},{64,80... | collective-permute-start | bytes 393224 | tf_op jit(solution)/shard_map/ppermute | solution.py:22
  83.6 4.0 %collective-permute-start.2 = (bf16[4,128,128]{2,1,0:T(8,128)(2,1)S(1)}, bf16[4,128,128]{2,1,0:T(8,128)(2,1)}, u32[]{:S(2)}, u32[]{:S(2)}) collective-permute-start(bf16[4,128,128]{2,1,0:T(8,128)(2,1)S(1)} %get-tuple-element.43), channel_id=1, source_target_pairs={{0,24},{8,32},{16,40},{24,48},{32,56},{40,0},{48,8},{56,16},{64,88... | collective-permute-start | bytes 393224 | tf_op jit(solution)/shard_map/ppermute | solution.py:22
  87.6 0.5 collective-permute-start.3
  88.1 5.0 %collective-permute-start.4 = (bf16[4,128,128]{2,1,0:T(8,128)(2,1)S(1)}, bf16[4,128,128]{2,1,0:T(8,128)(2,1)}, u32[]{:S(2)}, u32[]{:S(2)}) collective-permute-start(bf16[4,128,128]{2,1,0:T(8,128)(2,1)S(1)} %get-tuple-element.43), channel_id=1, source_target_pairs={{0,40},{8,48},{16,56},{24,0},{32,8},{40,16},{48,24},{56,32},{64,10... | collective-permute-start | bytes 393224 | tf_op jit(solution)/shard_map/ppermute | solution.py:22
  93.2 0.4 copy.18
  93.6 1.7 fusion.15
  95.3 2.7 %collective-permute-start.5 = (bf16[4,128,128]{2,1,0:T(8,128)(2,1)S(1)}, bf16[4,128,128]{2,1,0:T(8,128)(2,1)S(1)}, u32[]{:S(2)}, u32[]{:S(2)}) collective-permute-start(bf16[4,128,128]{2,1,0:T(8,128)(2,1)S(1)} %get-tuple-element.43), channel_id=1, source_target_pairs={{0,48},{8,56},{16,0},{24,8},{32,16},{40,24},{48,32},{56,40},{64,11... | collective-permute-start | bytes 393224 | tf_op jit(solution)/shard_map/ppermute | solution.py:22
  97.9 3.4 %collective-permute-start.6 = (bf16[4,128,128]{2,1,0:T(8,128)(2,1)S(1)}, bf16[4,128,128]{2,1,0:T(8,128)(2,1)S(1)}, u32[]{:S(2)}, u32[]{:S(2)}) collective-permute-start(bf16[4,128,128]{2,1,0:T(8,128)(2,1)S(1)} %get-tuple-element.43), channel_id=1, source_target_pairs={{0,56},{8,0},{16,8},{24,16},{32,24},{40,32},{48,40},{56,48},{64,12... | collective-permute-start | bytes 393224 | tf_op jit(solution)/shard_map/ppermute | solution.py:22
  101.4 3.8 %collective-permute-done.2 = bf16[4,128,128]{2,1,0:T(8,128)(2,1)} collective-permute-done((bf16[4,128,128]{2,1,0:T(8,128)(2,1)S(1)}, bf16[4,128,128]{2,1,0:T(8,128)(2,1)}, u32[]{:S(2)}, u32[]{:S(2)}) %collective-permute-start.2) | collective-permute-done | bytes 131104 | tf_op jit(solution)/shard_map/ppermute | solution.py:22
  105.2 3.8 %collective-permute-done.4 = bf16[4,128,128]{2,1,0:T(8,128)(2,1)} collective-permute-done((bf16[4,128,128]{2,1,0:T(8,128)(2,1)S(1)}, bf16[4,128,128]{2,1,0:T(8,128)(2,1)}, u32[]{:S(2)}, u32[]{:S(2)}) %collective-permute-start.4) | collective-permute-done | bytes 131104 | tf_op jit(solution)/shard_map/ppermute | solution.py:22
  109.0 2.1 %collective-permute-done.5 = bf16[4,128,128]{2,1,0:T(8,128)(2,1)S(1)} collective-permute-done((bf16[4,128,128]{2,1,0:T(8,128)(2,1)S(1)}, bf16[4,128,128]{2,1,0:T(8,128)(2,1)S(1)}, u32[]{:S(2)}, u32[]{:S(2)}) %collective-permute-start.5) | collective-permute-done | bytes 131104 | tf_op jit(solution)/shard_map/ppermute | solution.py:22
  111.1 1.5 collective-permute-done.6
  112.7 1.1 add_add_fusion
  113.7 1.7 collective-permute-start.7
  115.4 0.9 collective-permute-start.8
  116.3 2.4 %collective-permute-start.9 = (bf16[4,128,128]{2,1,0:T(8,128)(2,1)S(1)}, bf16[4,128,128]{2,1,0:T(8,128)(2,1)S(1)}, u32[]{:S(2)}, u32[]{:S(2)}) collective-permute-start(bf16[4,128,128]{2,1,0:T(8,128)(2,1)S(1)} %add_add_fusion), channel_id=1, source_target_pairs={{0,192},{8,200},{16,208},{24,216},{32,224},{40,232},{48,240},{56,2... | collective-permute-start | bytes 393224 | tf_op jit(solution)/shard_map/ppermute | solution.py:22
  118.8 0.9 bitcast_dynamic-update-slice_fusion.4
  119.7 0.9 bitcast_dynamic-update-slice_fusion.3
  120.7 0.9 bitcast_dynamic-update-slice_fusion.2
  121.6 0.7 fusion.16
  122.4 0.6 collective-permute-done.8
  123.0 0.7 collective-permute-done.9
  123.8 0.5 fusion.22
  124.4 0.5 fusion.30
  125.0 0.5 multiply_reduce_fusion
  125.5 0.2 multiply_convert_fusion
  125.7 0.3 copy.21
  126.0 6.5 %convolution_convert_fusion = bf16[512,4096]{1,0:T(8,128)(2,1)} fusion(bf16[512,4096]{1,0:T(8,128)(2,1)} %bitcast.189, bf16[64,8,4,128]{3,2,1,0:T(4,128)(2,1)S(1)} %bitcast.194), kind=kOutput, calls=%fused_computation.10 | convolution fusion | flops 2149580800 | bytes 8912896 | tf_op jit(solution)/shard_map/dot_general | solution.py:93
  132.6 37.9 %reduce-scatter.2.cloned.1.call-done = bf16[512,512]{1,0:T(8,128)(2,1)} async-done(((bf16[512,4096]{1,0:T(8,128)(2,1)}), bf16[512,512]{1,0:T(8,128)(2,1)}) %reduce-scatter.2.cloned.1.call-update) | async-done | bytes 524304 | tf_op jit(solution)/shard_map/reduce_scatter | solution.py:94
  (39 shorter events, 0.7 us)
Async XLA Ops:
  10.1 4.9 %copy-start.8 = (f32[4,4,4,4]{3,2,1,0:T(4,128)S(1)}, f32[4,4,4,4]{3,2,1,0:T(4,128)}, u32[]{:S(2)}) copy-start(f32[4,4,4,4]{3,2,1,0:T(4,128)} %param.8) | copy-start | bytes 3076
  10.2 4.9 %copy-start.2 = (bf16[3,4,1024,128]{3,2,1,0:T(8,128)(2,1)S(1)}, bf16[3,4,1024,128]{3,2,1,0:T(8,128)(2,1)}, u32[]{:S(2)}) copy-start(bf16[3,4,1024,128]{3,2,1,0:T(8,128)(2,1)} %param.6) | copy-start | bytes 9437188
  10.2 54.5 %all-to-all-start = ((bf16[8,512,512]{1,2,0:T(8,128)(2,1)}), bf16[8,512,512]{1,2,0:T(8,128)(2,1)}, u32[]{:S(2)}, u32[]{:S(2)}) async-start(bf16[8,512,512]{1,2,0:T(8,128)(2,1)} %stack.66), calls=%async_computation | async-start | bytes 8388608 | tf_op jit(solution)/shard_map/all_to_all | solution.py:55
  15.0 155.5 %reduce-scatter.2.cloned.1.call-start = ((), (), s32[]{:S(2)}) async-start(), calls=%async_computation.2 | async-start | bytes 4718592 | tf_op jit(solution)/shard_map/reduce_scatter | solution.py:94
  27.1 5.0 %copy-start = (bf16[4,1024,4,128]{3,2,1,0:T(4,128)(2,1)S(1)}, bf16[4,1024,4,128]{3,2,1,0:T(4,128)(2,1)}, u32[]{:S(2)}) copy-start(bf16[4,1024,4,128]{3,2,1,0:T(4,128)(2,1)} %get-tuple-element.48) | copy-start | bytes 12582916
  32.1 2.7 %copy-start.3 = (f32[1024,128]{1,0:T(8,128)S(1)}, f32[1024,128]{1,0:T(8,128)}, u32[]{:S(2)}) copy-start(f32[1024,128]{1,0:T(8,128)} %get-tuple-element.7) | copy-start | bytes 1572868
  32.1 2.7 %copy-start.4 = (f32[1024,128]{1,0:T(8,128)S(1)}, f32[1024,128]{1,0:T(8,128)}, u32[]{:S(2)}) copy-start(f32[1024,128]{1,0:T(8,128)} %get-tuple-element.14) | copy-start | bytes 1572868
  32.1 2.7 %copy-start.5 = (f32[1024,128]{1,0:T(8,128)S(1)}, f32[1024,128]{1,0:T(8,128)}, u32[]{:S(2)}) copy-start(f32[1024,128]{1,0:T(8,128)} %get-tuple-element.15) | copy-start | bytes 1572868
  32.1 2.7 %copy-start.6 = (f32[1024,128]{1,0:T(8,128)S(1)}, f32[1024,128]{1,0:T(8,128)}, u32[]{:S(2)}) copy-start(f32[1024,128]{1,0:T(8,128)} %get-tuple-element.16) | copy-start | bytes 1572868
  39.4 2.7 %copy-start.7 = (bf16[4,128,1024]{2,1,0:T(8,128)(2,1)S(1)}, bf16[4,128,1024]{2,1,0:T(8,128)(2,1)}, u32[]{:S(2)}) copy-start(bf16[4,128,1024]{2,1,0:T(8,128)(2,1)} %param.7) | copy-start | bytes 3145732
  78.3 17.0 %collective-permute-start = (bf16[4,128,128]{2,1,0:T(8,128)(2,1)S(1)}, bf16[4,128,128]{2,1,0:T(8,128)(2,1)S(1)}, u32[]{:S(2)}, u32[]{:S(2)}) collective-permute-start(bf16[4,128,128]{2,1,0:T(8,128)(2,1)S(1)} %get-tuple-element.43), channel_id=1, source_target_pairs={{0,8},{8,16},{16,24},{24,32},{32,40},{40,48},{48,56},{56,0},{64,72... | collective-permute-start | bytes 393224 | tf_op jit(solution)/shard_map/ppermute | solution.py:22
  80.3 17.6 %collective-permute-start.1 = (bf16[4,128,128]{2,1,0:T(8,128)(2,1)S(1)}, bf16[4,128,128]{2,1,0:T(8,128)(2,1)S(1)}, u32[]{:S(2)}, u32[]{:S(2)}) collective-permute-start(bf16[4,128,128]{2,1,0:T(8,128)(2,1)S(1)} %get-tuple-element.43), channel_id=1, source_target_pairs={{0,16},{8,24},{16,32},{24,40},{32,48},{40,56},{48,0},{56,8},{64,80... | collective-permute-start | bytes 393224 | tf_op jit(solution)/shard_map/ppermute | solution.py:22
  83.6 21.6 %collective-permute-start.2 = (bf16[4,128,128]{2,1,0:T(8,128)(2,1)S(1)}, bf16[4,128,128]{2,1,0:T(8,128)(2,1)}, u32[]{:S(2)}, u32[]{:S(2)}) collective-permute-start(bf16[4,128,128]{2,1,0:T(8,128)(2,1)S(1)} %get-tuple-element.43), channel_id=1, source_target_pairs={{0,24},{8,32},{16,40},{24,48},{32,56},{40,0},{48,8},{56,16},{64,88... | collective-permute-start | bytes 393224 | tf_op jit(solution)/shard_map/ppermute | solution.py:22
  87.6 17.6 %collective-permute-start.3 = (bf16[4,128,128]{2,1,0:T(8,128)(2,1)S(1)}, bf16[4,128,128]{2,1,0:T(8,128)(2,1)}, u32[]{:S(2)}, u32[]{:S(2)}) collective-permute-start(bf16[4,128,128]{2,1,0:T(8,128)(2,1)S(1)} %get-tuple-element.43), channel_id=1, source_target_pairs={{0,32},{8,40},{16,48},{24,56},{32,0},{40,8},{48,16},{56,24},{64,96... | collective-permute-start | bytes 393224 | tf_op jit(solution)/shard_map/ppermute | solution.py:22
  88.1 20.9 %collective-permute-start.4 = (bf16[4,128,128]{2,1,0:T(8,128)(2,1)S(1)}, bf16[4,128,128]{2,1,0:T(8,128)(2,1)}, u32[]{:S(2)}, u32[]{:S(2)}) collective-permute-start(bf16[4,128,128]{2,1,0:T(8,128)(2,1)S(1)} %get-tuple-element.43), channel_id=1, source_target_pairs={{0,40},{8,48},{16,56},{24,0},{32,8},{40,16},{48,24},{56,32},{64,10... | collective-permute-start | bytes 393224 | tf_op jit(solution)/shard_map/ppermute | solution.py:22
  95.3 15.9 %collective-permute-start.5 = (bf16[4,128,128]{2,1,0:T(8,128)(2,1)S(1)}, bf16[4,128,128]{2,1,0:T(8,128)(2,1)S(1)}, u32[]{:S(2)}, u32[]{:S(2)}) collective-permute-start(bf16[4,128,128]{2,1,0:T(8,128)(2,1)S(1)} %get-tuple-element.43), channel_id=1, source_target_pairs={{0,48},{8,56},{16,0},{24,8},{32,16},{40,24},{48,32},{56,40},{64,11... | collective-permute-start | bytes 393224 | tf_op jit(solution)/shard_map/ppermute | solution.py:22
  97.9 14.7 %collective-permute-start.6 = (bf16[4,128,128]{2,1,0:T(8,128)(2,1)S(1)}, bf16[4,128,128]{2,1,0:T(8,128)(2,1)S(1)}, u32[]{:S(2)}, u32[]{:S(2)}) collective-permute-start(bf16[4,128,128]{2,1,0:T(8,128)(2,1)S(1)} %get-tuple-element.43), channel_id=1, source_target_pairs={{0,56},{8,0},{16,8},{24,16},{32,24},{40,32},{48,40},{56,48},{64,12... | collective-permute-start | bytes 393224 | tf_op jit(solution)/shard_map/ppermute | solution.py:22
  113.7 8.6 %collective-permute-start.7 = (bf16[4,128,128]{2,1,0:T(8,128)(2,1)S(1)}, bf16[4,128,128]{2,1,0:T(8,128)(2,1)S(1)}, u32[]{:S(2)}, u32[]{:S(2)}) collective-permute-start(bf16[4,128,128]{2,1,0:T(8,128)(2,1)S(1)} %add_add_fusion), channel_id=1, source_target_pairs={{0,64},{8,72},{16,80},{24,88},{32,96},{40,104},{48,112},{56,120},{... | collective-permute-start | bytes 393224 | tf_op jit(solution)/shard_map/ppermute | solution.py:22
  115.4 7.6 %collective-permute-start.8 = (bf16[4,128,128]{2,1,0:T(8,128)(2,1)S(1)}, bf16[4,128,128]{2,1,0:T(8,128)(2,1)S(1)}, u32[]{:S(2)}, u32[]{:S(2)}) collective-permute-start(bf16[4,128,128]{2,1,0:T(8,128)(2,1)S(1)} %add_add_fusion), channel_id=1, source_target_pairs={{0,128},{8,136},{16,144},{24,152},{32,160},{40,168},{48,176},{56,1... | collective-permute-start | bytes 393224 | tf_op jit(solution)/shard_map/ppermute | solution.py:22
  116.3 7.4 %collective-permute-start.9 = (bf16[4,128,128]{2,1,0:T(8,128)(2,1)S(1)}, bf16[4,128,128]{2,1,0:T(8,128)(2,1)S(1)}, u32[]{:S(2)}, u32[]{:S(2)}) collective-permute-start(bf16[4,128,128]{2,1,0:T(8,128)(2,1)S(1)} %add_add_fusion), channel_id=1, source_target_pairs={{0,192},{8,200},{16,208},{24,216},{32,224},{40,232},{48,240},{56,2... | collective-permute-start | bytes 393224 | tf_op jit(solution)/shard_map/ppermute | solution.py:22
  121.6 3.3 %copy-start.1 = (f32[4,4,128,128]{3,2,1,0:T(8,128)S(1)}, f32[4,4,128,128]{3,2,1,0:T(8,128)}, u32[]{:S(2)}) copy-start(f32[4,4,128,128]{3,2,1,0:T(8,128)} %fusion.15) | copy-start | bytes 3145732
  124.4 1.2 copy-start.9
Sparse Core Ops, SparseCore 0:
  132.7 37.7 reduce-scatter.1
